TPU v7x, 32 devices: a whole 2x2x4 slice. The times are simulated.
32 devices in a mesh: groups: 2 (over y), feat: 4 (over z), tower: 4 (over x, core).
Axes of the slice: x: 2, y: 2, z: 4, core: 2. Of those that a mesh axis runs over, the one named last changes fastest.
Arguments:
- pooled_first: bfloat16 [4, 16, 3072, 128], P('tower', 'feat', 'groups'), parts along dimension 2, may hold values from -6 to 6
- pooled_second: bfloat16 [4, 16, 3072, 128], P('tower', 'feat', 'groups'), parts along dimension 2, may hold values from -6 to 6
- feature_order: int32 [4, 32], P('tower'), may hold values from 0 to 31, each once within a row
- cross_down: bfloat16 [4, 4096, 256], P('tower', 'feat'), may hold values from -0.09375 to 0.09375
- cross_up: bfloat16 [4, 4096, 256], P('tower', 'feat'), may hold values from -0.375 to 0.375
- cross_bias: float32 [4, 4096], P('tower'), may hold values from -3 to 3
- compress_weight: bfloat16 [4, 4096, 512], P('tower', 'feat'), may hold values from -0.09375 to 0.09375
- compress_bias: float32 [4, 512], P('tower'), may hold values from -3 to 3
- dense_vector: bfloat16 [3072, 128], P(('groups', 'feat', 'tower')), parts along dimension 0, may hold values from -6 to 6
- mlp_weight: bfloat16 [248, 1024], P('tower'), may hold values from -0.375 to 0.375
- mlp_bias: float32 [1024], replicated, may hold values from -3 to 3
Outputs:
- top_hidden: bfloat16 [3072, 1024], P(('groups', 'feat', 'tower')), parts along dimension 0
There are 2 independent parts, one for each index of `groups`. A program takes and returns all parts, laid end to end along the dimension named above; an argument that names none is the same for every part. Nothing has to cross between parts.
Inputs may be any that keep to these rules, and one draw needn't show every extreme that they name: Each row of feature_order names every number from 0 to 31 once.
All inputs are finite; a program needn't handle non-finite values.
Results may differ from a plain program's by a relative error of at most 0.0072.
Values may be sent and summed in bfloat16 or wider, within the bound.
No kernel may reach another device: no remote copies, remote signals or barrier semaphores. Data moves between devices by JAX's collectives and lax.ppermute only.
A program may use at most 64 MiB of HBM per device.

v0:
```python
import math
import jax
import jax.numpy as jnp
import numpy as np
from jax import lax
from jax.sharding import PartitionSpec as P


def pair_positions(vector_count):
    upper_rows, upper_cols = np.triu_indices(vector_count, 1)
    return upper_rows * vector_count + upper_cols


def on_device(
    pooled_first,
    pooled_second,
    feature_order,
    cross_down,
    cross_up,
    cross_bias,
    compress_weight,
    compress_bias,
    dense_vector,
    mlp_weight,
    mlp_bias,
):
    group_one, group_two = (
        lax.all_to_all(pooled_first, "feat", split_axis=2, concat_axis=1, tiled=True),
        lax.all_to_all(pooled_second, "feat", split_axis=2, concat_axis=1, tiled=True),
    )
    slot_data = jnp.concatenate([group_one[0], group_two[0]], 0)
    slot_count = slot_data.shape[0]
    row_count = slot_data.shape[1]
    entry_count = slot_data.shape[2]
    orders = feature_order[0]
    one_hot = (orders[None, :] == jnp.arange(slot_count, dtype=jnp.int32)[:, None]).astype(
        jnp.bfloat16
    )
    base_rows = jnp.einsum("fs,sre->rfe", one_hot, slot_data, preferred_element_type=jnp.float32)
    base_rows = base_rows.astype(jnp.bfloat16).reshape(row_count, slot_count * entry_count)
    weight_piece = lax.all_gather(cross_down[0], "feat", axis=0, tiled=True)
    columns = base_rows
    low_sum = jnp.dot(columns, weight_piece, preferred_element_type=jnp.float32)
    low_rank = low_sum.astype(jnp.bfloat16)
    shift_row = cross_bias[0]
    up_piece = lax.all_gather(cross_up[0], "feat", axis=0, tiled=True)
    squeeze_piece = lax.all_gather(compress_weight[0], "feat", axis=0, tiled=True)
    lifted = lax.dot_general(
        low_rank, up_piece, (((1,), (1,)), ((), ())), preferred_element_type=jnp.float32
    )
    columns = base_rows.astype(jnp.float32)
    crossed = (columns * (lifted + shift_row[None, :]) + columns).astype(jnp.bfloat16)
    squeezed = jnp.dot(crossed, squeeze_piece, preferred_element_type=jnp.float32)
    compressed = (squeezed + compress_bias[0][None, :]).astype(jnp.bfloat16)
    gathered = lax.all_to_all(compressed, "tower", split_axis=0, concat_axis=1, tiled=True)
    local_rows = gathered.shape[0]
    vector_count = gathered.shape[1] // entry_count
    vectors = gathered.reshape(local_rows, vector_count, entry_count)
    gram_matrix = jnp.einsum(
        "bie,bje->bij", vectors, vectors, preferred_element_type=jnp.float32
    ) * (1.0 / math.sqrt(entry_count))
    pair_terms = gram_matrix.reshape(local_rows, vector_count * vector_count)[
        :, pair_positions(vector_count)
    ]
    joined = jnp.concatenate([dense_vector.astype(jnp.float32), pair_terms], 1).astype(jnp.bfloat16)
    hidden_units = mlp_weight.shape[1]
    weight_piece = lax.all_gather(mlp_weight, "tower", axis=0, tiled=True)
    width_here = weight_piece.shape[0]
    columns = lax.slice_in_dim(joined, 0, width_here, axis=1)
    hidden_sum = jnp.zeros((local_rows, hidden_units), jnp.float32) + jnp.dot(
        columns, weight_piece, preferred_element_type=jnp.float32
    )
    return jax.nn.relu(hidden_sum + mlp_bias[None, :]).astype(jnp.bfloat16)


def solution(mesh):
    in_specs = (
        P("tower", "feat", "groups", None),
        P("tower", "feat", "groups", None),
        P("tower", None),
        P("tower", "feat", None),
        P("tower", "feat", None),
        P("tower", None),
        P("tower", "feat", None),
        P("tower", None),
        P(("groups", "feat", "tower"), None),
        P("tower", None),
        P(),
    )
    out_specs = P(("groups", "feat", "tower"), None)
    return jax.shard_map(
        on_device, mesh=mesh, in_specs=in_specs, out_specs=out_specs, check_vma=False
    )
```

profile of v0, /device:TPU:0, one launch (start us, length us, event | category | flops | bytes accessed | tf_op | source)
XLA Modules:
  0.0 278.5 jit_solution(6813317362227992565)
XLA Ops:
  6.5 0.7 all-gather.8.cloned.1.call-update
  7.3 0.0 all-gather.10.cloned.1.call-start
  7.3 0.7 all-gather.10.cloned.1.call-update
  8.0 0.0 all-gather.12.cloned.1.call-start
  8.1 0.7 all-gather.12.cloned.1.call-update
  8.7 0.0 copy-done.2
  8.8 8.2 %copy.24 = bf16[1,4,1536,128]{3,1,0,2:T(4,128)(2,1)} copy(bf16[1,4,1536,128]{3,2,1,0:T(8,128)(2,1)S(1)} %copy-done.2) | data formatting | bytes 3145728 | tf_op args[0]
  17.0 6.3 %all-to-all-start = ((bf16[1,4,1536,128]{3,1,0,2:T(4,128)(2,1)}), bf16[1,4,1536,128]{3,1,0,2:T(4,128)(2,1)S(1)}, u32[]{:S(2)}, u32[]{:S(2)}) async-start(bf16[1,4,1536,128]{3,1,0,2:T(4,128)(2,1)} %copy.24), calls=%async_computation | async-start | bytes 3145728 | tf_op jit(solution)/shard_map/all_to_all | solution.py:28
  23.3 8.2 %copy.26 = bf16[1,4,1536,128]{3,1,0,2:T(4,128)(2,1)} copy(bf16[1,4,1536,128]{3,2,1,0:T(8,128)(2,1)S(1)} %copy-done.3) | data formatting | bytes 3145728 | tf_op args[1]
  31.5 59.2 %all-to-all-done = bf16[1,4,1536,128]{3,1,0,2:T(4,128)(2,1)S(1)} async-done(((bf16[1,4,1536,128]{3,1,0,2:T(4,128)(2,1)}), bf16[1,4,1536,128]{3,1,0,2:T(4,128)(2,1)S(1)}, u32[]{:S(2)}, u32[]{:S(2)}) %all-to-all-start) | async-done | bytes 1572896 | tf_op jit(solution)/shard_map/all_to_all | solution.py:28
  90.7 3.7 %all-to-all-start.1 = ((bf16[1,4,1536,128]{3,1,0,2:T(4,128)(2,1)}), bf16[1,4,1536,128]{3,1,0,2:T(4,128)(2,1)S(1)}, u32[]{:S(2)}, u32[]{:S(2)}) async-start(bf16[1,4,1536,128]{3,1,0,2:T(4,128)(2,1)} %copy.26), calls=%async_computation.1 | async-start | bytes 3145728 | tf_op jit(solution)/shard_map/all_to_all | solution.py:29
  94.5 0.0 copy-start.7
  94.5 1.7 copy.25
  96.2 69.1 %all-to-all-done.1 = bf16[1,4,1536,128]{3,1,0,2:T(4,128)(2,1)S(1)} async-done(((bf16[1,4,1536,128]{3,1,0,2:T(4,128)(2,1)}), bf16[1,4,1536,128]{3,1,0,2:T(4,128)(2,1)S(1)}, u32[]{:S(2)}, u32[]{:S(2)}) %all-to-all-start.1) | async-done | bytes 1572896 | tf_op jit(solution)/shard_map/all_to_all | solution.py:29
  165.3 0.5 copy.27
  165.9 2.6 fusion.10
  168.5 3.8 %fusion.23 = bf16[384,256]{1,0:T(8,128)(2,1)S(1)} fusion(bf16[1,4096,256]{2,1,0:T(8,128)(2,1)} %all-gather.8.cloned.1.call-done, bf16[48,8,32,128]{3,2,1,0:T(8,128)(2,1)} %bitcast.56), kind=kOutput, calls=%fused_computation.21 | convolution fusion | flops 805404672 | bytes 5439488 | tf_op jit(solution)/shard_map/dot_general | solution.py:43
  172.3 0.0 all-gather.10.cloned.1.call-done
  172.3 74.9 %all-gather.12.cloned.1.call-done = bf16[1,4096,512]{2,1,0:T(8,128)(2,1)} async-done(((bf16[1,1024,512]{2,1,0:T(8,128)(2,1)}), bf16[1,4096,512]{2,1,0:T(8,128)(2,1)}) %all-gather.12.cloned.1.call-update) | async-done | bytes 4194320 | tf_op jit(solution)/shard_map/all_gather | solution.py:47
  247.2 0.0 copy-start.8
  247.2 7.0 %fusion.18 = bf16[384,512]{1,0:T(8,128)(2,1)} fusion(bf16[1,4096,512]{2,1,0:T(8,128)(2,1)} %all-gather.12.cloned.1.call-done, bf16[384,256]{1,0:T(8,128)(2,1)S(1)} %fusion.23, f32[4096]{0:T(1024)S(1)} %bitcast.63, bf16[48,8,32,128]{3,2,1,0:T(8,128)(2,1)S(1)} %bitcast.57, bf16[1,4096,256]{2,1,0:T(8,128)(2,1)} %all-gather.10.cloned.1.call-done, ...), kind=kOutput, calls=%fused_computation.17 | convolution fusion | flops 2424176640 | bytes 10045440 | tf_op jit(solution)/shard_map/dot_general | solution.py:53
  254.2 3.6 %all-to-all-start.2 = ((bf16[4,96,512]{2,1,0:T(8,128)(2,1)}), bf16[4,96,512]{2,1,0:T(8,128)(2,1)S(1)}, u32[]{:S(2)}, u32[]{:S(2)}) async-start(bf16[4,96,512]{2,1,0:T(8,128)(2,1)} %bitcast.14), calls=%async_computation.2 | async-start | bytes 786432 | tf_op jit(solution)/shard_map/all_to_all | solution.py:55
  257.8 11.1 %all-gather.3 = bf16[4,62,1024]{2,1,0:T(8,128)(2,1)S(1)} all-gather(bf16[1,62,1024]{2,1,0:T(8,128)(2,1)S(1)} %bitcast.60), channel_id=1, replica_groups=mesh['groups'=2,'feat'=4,'tower'=4] {'tower'}, dimensions={0}, use_global_device_ids=true | all-gather | bytes 634880 | tf_op jit(solution)/shard_map/all_gather | solution.py:67
  268.9 0.1 reshape.31
  269.1 0.0 all-to-all-done.2
  269.1 0.3 copy.28
  269.4 0.2 reshape.17
  269.5 0.3 convolution_multiply_fusion
  269.9 0.3 copy.29
  270.2 0.7 gather_fusion
  270.9 0.1 copy.30
  271.1 0.9 fusion.22
  (22 shorter events, 0.0 us)
Async XLA Ops:
  6.5 2.2 copy-start.2
  6.5 162.0 %all-gather.8.cloned.1.call-start = ((), (), s32[]{:S(2)}) async-start(), calls=%async_computation.3 | async-start | bytes 2621440 | tf_op jit(solution)/shard_map/all_gather | solution.py:41
  7.3 165.0 %all-gather.10.cloned.1.call-start = ((), (), s32[]{:S(2)}) async-start(), calls=%async_computation.4 | async-start | bytes 2621440 | tf_op jit(solution)/shard_map/all_gather | solution.py:46
  8.0 239.2 %all-gather.12.cloned.1.call-start = ((), (), s32[]{:S(2)}) async-start(), calls=%async_computation.5 | async-start | bytes 5242880 | tf_op jit(solution)/shard_map/all_gather | solution.py:47
  8.8 14.5 %copy-start.3 = (bf16[1,4,1536,128]{3,2,1,0:T(8,128)(2,1)S(1)}, bf16[1,4,1536,128]{3,2,1,0:T(8,128)(2,1)}, u32[]{:S(2)}) copy-start(bf16[1,4,1536,128]{3,2,1,0:T(8,128)(2,1)} %param.14) | copy-start | bytes 4718596
  17.0 73.7 %all-to-all-start = ((bf16[1,4,1536,128]{3,1,0,2:T(4,128)(2,1)}), bf16[1,4,1536,128]{3,1,0,2:T(4,128)(2,1)S(1)}, u32[]{:S(2)}, u32[]{:S(2)}) async-start(bf16[1,4,1536,128]{3,1,0,2:T(4,128)(2,1)} %copy.24), calls=%async_computation | async-start | bytes 3145728 | tf_op jit(solution)/shard_map/all_to_all | solution.py:28
  90.7 74.6 %all-to-all-start.1 = ((bf16[1,4,1536,128]{3,1,0,2:T(4,128)(2,1)}), bf16[1,4,1536,128]{3,1,0,2:T(4,128)(2,1)S(1)}, u32[]{:S(2)}, u32[]{:S(2)}) async-start(bf16[1,4,1536,128]{3,1,0,2:T(4,128)(2,1)} %copy.26), calls=%async_computation.1 | async-start | bytes 3145728 | tf_op jit(solution)/shard_map/all_to_all | solution.py:29
  94.5 71.4 %copy-start.7 = (s32[1,32]{1,0:T(1,128)S(1)}, s32[1,32]{1,0:T(1,128)}, u32[]{:S(2)}) copy-start(s32[1,32]{1,0:T(1,128)} %param.15) | copy-start | bytes 388
  96.2 69.7 %copy-start = (bf16[1,4,4,384,128]{4,1,2,3,0:T(4,128)(2,1)S(1)}, bf16[1,4,4,384,128]{4,1,2,3,0:T(4,128)(2,1)}, u32[]{:S(2)}) copy-start(bf16[1,4,4,384,128]{4,1,2,3,0:T(4,128)(2,1)} %copy.25) | copy-start | bytes 4718596
  168.5 78.7 %copy-start.1 = (bf16[384,128,32]{1,2,0:T(8,128)(2,1)S(1)}, bf16[384,128,32]{1,2,0:T(8,128)(2,1)}, u32[]{:S(2)}) copy-start(bf16[384,128,32]{1,2,0:T(8,128)(2,1)} %fusion.10) | copy-start | bytes 9437188
  168.5 78.7 %copy-start.9 = (f32[1,4096]{1,0:T(1,128)S(1)}, f32[1,4096]{1,0:T(1,128)}, u32[]{:S(2)}) copy-start(f32[1,4096]{1,0:T(1,128)} %param.18) | copy-start | bytes 49156
  168.5 78.7 %copy-start.10 = (f32[1,512]{1,0:T(1,128)S(1)}, f32[1,512]{1,0:T(1,128)}, u32[]{:S(2)}) copy-start(f32[1,512]{1,0:T(1,128)} %param.20) | copy-start | bytes 6148
  247.2 10.6 %copy-start.4 = (bf16[62,1024]{1,0:T(8,128)(2,1)S(1)}, bf16[62,1024]{1,0:T(8,128)(2,1)}, u32[]{:S(2)}) copy-start(bf16[62,1024]{1,0:T(8,128)(2,1)} %param.22) | copy-start | bytes 380932
  247.2 21.8 %copy-start.8 = (s32[120]{0:T(128)S(1)}, s32[120]{0:T(128)}, u32[]{:S(2)}) copy-start(s32[120]{0:T(128)} %constant.23) | copy-start | bytes 1444
  254.2 16.8 %copy-start.5 = (bf16[96,128]{1,0:T(8,128)(2,1)S(1)}, bf16[96,128]{1,0:T(8,128)(2,1)}, u32[]{:S(2)}) copy-start(bf16[96,128]{1,0:T(8,128)(2,1)} %param.21) | copy-start | bytes 73732
  254.2 16.8 %copy-start.6 = (f32[1024]{0:T(1024)S(1)}, f32[1024]{0:T(1024)}, u32[]{:S(2)}) copy-start(f32[1024]{0:T(1024)} %param.23) | copy-start | bytes 12292
  254.2 14.8 %all-to-all-start.2 = ((bf16[4,96,512]{2,1,0:T(8,128)(2,1)}), bf16[4,96,512]{2,1,0:T(8,128)(2,1)S(1)}, u32[]{:S(2)}, u32[]{:S(2)}) async-start(bf16[4,96,512]{2,1,0:T(8,128)(2,1)} %bitcast.14), calls=%async_computation.2 | async-start | bytes 786432 | tf_op jit(solution)/shard_map/all_to_all | solution.py:55
Sparse Core Ops, SparseCore 0:
  8.9 80.3 all-gather.7
  90.9 74.7 all-gather.9
  167.3 79.9 all-gather.11
where the time goes:
time: 279 us
  waiting for transfers between devices  205 us (73%)
  local copies, waits for them, and re-layouts  20.4 us (7%)
  matrix products  14.6 us (5%)
  starting transfers between devices  13.7 us (5%)
  between operations  13.3 us (5%)
  blocking collectives  11.1 us (4%)
    all_gather x1, waiting for transfers between devices, on_device(): lax.all_gather(compress_weight[0], 'feat', axis=0, tiled=True)  74.9 us
    all_to_all x1, waiting for transfers between devices, on_device(): lax.all_to_all(pooled_second, 'feat', split_axis=2, concat_axis=1, tiled=...  69.1 us
    all_to_all x1, waiting for transfers between devices, on_device(): lax.all_to_all(pooled_first, 'feat', split_axis=2, concat_axis=1, tiled=T...  59.2 us
    unnamed x25, local copies, waits for them, and re-layouts  16.6 us
    all_gather x1, blocking collectives, on_device(): weight_piece = lax.all_gather(mlp_weight, 'tower', axis=0, tiled=True)  11.1 us
    dot_general x1, matrix products, on_device(): jnp.dot(crossed, squeeze_piece, preferred_element_type=jnp.float32)  6.96 us
    all_to_all x1, starting transfers between devices, on_device(): lax.all_to_all(pooled_first, 'feat', split_axis=2, concat_axis=1, tiled=T...  6.32 us
  transfers between devices with their start and end apart: 6, of which 3 were waited for; matrix products, arithmetic and copies ran while one was open for 9% of the time, Pallas kernels for 0%

commit v1 on v0

--- a/solution.py
+++ b/solution.py
@@ -4,6 +4,18 @@
 import numpy as np
 from jax import lax
 from jax.sharding import PartitionSpec as P
+
+
+def rotated_exchange(value, axis, split, join):
+    ways, here = (lax.axis_size(axis), lax.axis_index(axis))
+    width = value.shape[split] // ways
+    turned = jnp.roll(value, -here * width, axis=split)
+    got = [lax.slice_in_dim(turned, 0, width, axis=split)]
+    for far in range(1, ways):
+        sent = lax.slice_in_dim(turned, far * width, (far + 1) * width, axis=split)
+        got.append(lax.ppermute(sent, axis, [(d, (d + far) % ways) for d in range(ways)]))
+    line = jnp.concatenate(got[::-1], axis=join)
+    return jnp.roll(line, (here + 1) * got[0].shape[join], axis=join)
 
 
 def pair_positions(vector_count):
@@ -25,7 +37,7 @@
     mlp_bias,
 ):
     group_one, group_two = (
-        lax.all_to_all(pooled_first, "feat", split_axis=2, concat_axis=1, tiled=True),
+        rotated_exchange(pooled_first, "feat", 2, 1),
         lax.all_to_all(pooled_second, "feat", split_axis=2, concat_axis=1, tiled=True),
     )
     slot_data = jnp.concatenate([group_one[0], group_two[0]], 0)

time: 279 us -> 271 us (0.971)
  waiting for transfers between devices: 205 us -> 197 us
  local copies, waits for them, and re-layouts: 20.4 us -> 17.2 us
    ppermute x0 -> x3, waiting for transfers between devices: none -> 110 us  [rotated_exchange(): lax.ppermute(sent, axis, [(d, (d + far) % ways) for d in range(ways)])]
    all_to_all x1, waiting for transfers between devices: 69.1 us -> 0.01 us  [on_device(): lax.all_to_all(pooled_second, 'feat', split_axis=2, concat_axis=1, tiled=...]
    all_to_all x1 -> x0, waiting for transfers between devices: 59.2 us -> none  [on_device(): lax.all_to_all(pooled_first, 'feat', split_axis=2, concat_axis=1, tiled=T...]
    all_to_all x1 -> x0, starting transfers between devices: 6.32 us -> none  [on_device(): lax.all_to_all(pooled_first, 'feat', split_axis=2, concat_axis=1, tiled=T...]
    all_gather x1, waiting for transfers between devices: 74.9 us -> 80.8 us  [on_device(): lax.all_gather(compress_weight[0], 'feat', axis=0, tiled=True)]
    ppermute x0 -> x3, starting transfers between devices: none -> 4.91 us  [rotated_exchange(): lax.ppermute(sent, axis, [(d, (d + far) % ways) for d in range(ways)])]
    all_gather x1, waiting for transfers between devices: 0.02 us -> 3.94 us  [on_device(): up_piece = lax.all_gather(cross_up[0], 'feat', axis=0, tiled=True)]
    unnamed x25 -> x27, local copies, waits for them, and re-layouts: 16.6 us -> 12.7 us
  transfers between devices with their start and end apart: 6 -> 8, of which waited for: 3 -> 4; matrix products, arithmetic and copies ran while one was open for 9% -> 9% of each run, Pallas kernels for 0% -> 0%
where the time goes in v1:
time: 271 us
  waiting for transfers between devices  197 us (73%)
  local copies, waits for them, and re-layouts  17.2 us (6%)
  starting transfers between devices  14.9 us (5%)
  matrix products  14.6 us (5%)
  between operations  13.3 us (5%)
  blocking collectives  11.1 us (4%)
    ppermute x3, waiting for transfers between devices, rotated_exchange(): lax.ppermute(sent, axis, [(d, (d + far) % ways) for d in range(ways)])  110 us
    all_gather x1, waiting for transfers between devices, on_device(): lax.all_gather(compress_weight[0], 'feat', axis=0, tiled=True)  80.8 us
    unnamed x27, local copies, waits for them, and re-layouts  12.7 us
    all_gather x1, blocking collectives, on_device(): weight_piece = lax.all_gather(mlp_weight, 'tower', axis=0, tiled=True)  11.1 us
    dot_general x1, matrix products, on_device(): jnp.dot(crossed, squeeze_piece, preferred_element_type=jnp.float32)  6.96 us
    all_to_all x1, starting transfers between devices, on_device(): lax.all_to_all(pooled_second, 'feat', split_axis=2, concat_axis=1, tiled=...  6.32 us
  transfers between devices with their start and end apart: 8, of which 4 were waited for; matrix products, arithmetic and copies ran while one was open for 9% of the time, Pallas kernels for 0%

profile of v1, /device:TPU:0, one launch (start us, length us, event | category | flops | bytes accessed | tf_op | source)
XLA Modules:
  0.0 270.9 jit_solution(6861667365991207996)
XLA Ops:
  6.5 0.7 all-gather.8.cloned.1.call-update
  7.3 0.7 all-gather.10.cloned.1.call-update
  8.1 0.7 all-gather.12.cloned.1.call-update
  8.8 8.2 %copy.25 = bf16[1,4,1536,128]{3,1,0,2:T(4,128)(2,1)} copy(bf16[1,4,1536,128]{3,2,1,0:T(8,128)(2,1)S(1)} %copy-done.1) | data formatting | bytes 3145728 | tf_op args[1]
  17.0 6.3 %all-to-all-start = ((bf16[1,4,1536,128]{3,1,0,2:T(4,128)(2,1)}), bf16[1,4,1536,128]{3,1,0,2:T(4,128)(2,1)S(1)}, u32[]{:S(2)}, u32[]{:S(2)}) async-start(bf16[1,4,1536,128]{3,1,0,2:T(4,128)(2,1)} %copy.25), calls=%async_computation | async-start | bytes 3145728 | tf_op jit(solution)/shard_map/all_to_all | solution.py:41
  23.3 2.5 fusion.15
  25.8 1.1 fusion.39
  26.9 3.8 %collective-permute-start = (bf16[1,4,384,128]{3,2,1,0:T(8,128)(2,1)}, bf16[1,4,384,128]{3,2,1,0:T(8,128)(2,1)S(1)}, u32[]{:S(2)}, u32[]{:S(2)}) collective-permute-start(bf16[1,4,384,128]{3,2,1,0:T(8,128)(2,1)} %get-tuple-element.7), channel_id=1, source_target_pairs={{0,12},{4,0},{8,4},{12,8},{1,13},{5,1},{9,5},{13,9},{2,14},{6,2},{... | collective-permute-start | bytes 1179656 | tf_op jit(solution)/shard_map/ppermute | solution.py:16
  30.8 1.1 collective-permute-start.2
  31.9 55.9 %collective-permute-done = bf16[1,4,384,128]{3,2,1,0:T(8,128)(2,1)S(1)} collective-permute-done((bf16[1,4,384,128]{3,2,1,0:T(8,128)(2,1)}, bf16[1,4,384,128]{3,2,1,0:T(8,128)(2,1)S(1)}, u32[]{:S(2)}, u32[]{:S(2)}) %collective-permute-start) | collective-permute-done | bytes 393248 | tf_op jit(solution)/shard_map/ppermute | solution.py:16
  87.8 54.4 %collective-permute-done.1 = bf16[1,4,384,128]{3,2,1,0:T(8,128)(2,1)} collective-permute-done((bf16[1,4,384,128]{3,2,1,0:T(8,128)(2,1)}, bf16[1,4,384,128]{3,2,1,0:T(8,128)(2,1)}, u32[]{:S(2)}, u32[]{:S(2)}) %collective-permute-start.1) | collective-permute-done | bytes 393248 | tf_op jit(solution)/shard_map/ppermute | solution.py:16
  142.2 1.0 constant_dynamic-update-slice_fusion.4
  143.3 1.0 constant_dynamic-update-slice_fusion.3
  144.5 1.0 constant_dynamic-update-slice_fusion.1
  145.5 1.0 constant_dynamic-update-slice_fusion
  146.6 0.1 constant_dynamic-slice_fusion
  146.8 1.0 copy.41
  147.9 0.5 copy.26
  148.4 2.6 fusion.10
  151.1 3.8 %fusion.24 = bf16[384,256]{1,0:T(8,128)(2,1)S(1)} fusion(bf16[1,4096,256]{2,1,0:T(8,128)(2,1)} %all-gather.8.cloned.1.call-done, bf16[48,8,32,128]{3,2,1,0:T(8,128)(2,1)} %bitcast.54), kind=kOutput, calls=%fused_computation.25 | convolution fusion | flops 805404672 | bytes 5439488 | tf_op jit(solution)/shard_map/dot_general | solution.py:55
  154.9 3.9 %all-gather.10.cloned.1.call-done = bf16[1,4096,256]{2,1,0:T(8,128)(2,1)} async-done(((bf16[1,1024,256]{2,1,0:T(8,128)(2,1)}), bf16[1,4096,256]{2,1,0:T(8,128)(2,1)}) %all-gather.10.cloned.1.call-update) | async-done | bytes 2097168 | tf_op jit(solution)/shard_map/all_gather | solution.py:58
  158.8 80.8 %all-gather.12.cloned.1.call-done = bf16[1,4096,512]{2,1,0:T(8,128)(2,1)} async-done(((bf16[1,1024,512]{2,1,0:T(8,128)(2,1)}), bf16[1,4096,512]{2,1,0:T(8,128)(2,1)}) %all-gather.12.cloned.1.call-update) | async-done | bytes 4194320 | tf_op jit(solution)/shard_map/all_gather | solution.py:59
  239.6 7.0 %fusion.19 = bf16[384,512]{1,0:T(8,128)(2,1)} fusion(bf16[1,4096,512]{2,1,0:T(8,128)(2,1)} %all-gather.12.cloned.1.call-done, bf16[384,256]{1,0:T(8,128)(2,1)S(1)} %fusion.24, f32[4096]{0:T(1024)S(1)} %bitcast.61, bf16[48,8,32,128]{3,2,1,0:T(8,128)(2,1)S(1)} %bitcast.55, bf16[1,4096,256]{2,1,0:T(8,128)(2,1)} %all-gather.10.cloned.1.call-done, ...), kind=kOutput, calls=%fused_computation.21 | convolution fusion | flops 2424176640 | bytes 10045440 | tf_op jit(solution)/shard_map/dot_general | solution.py:65
  246.6 3.6 %all-to-all-start.1 = ((bf16[4,96,512]{2,1,0:T(8,128)(2,1)}), bf16[4,96,512]{2,1,0:T(8,128)(2,1)S(1)}, u32[]{:S(2)}, u32[]{:S(2)}) async-start(bf16[4,96,512]{2,1,0:T(8,128)(2,1)} %bitcast.12), calls=%async_computation.1 | async-start | bytes 786432 | tf_op jit(solution)/shard_map/all_to_all | solution.py:67
  250.2 11.1 %all-gather.3 = bf16[4,62,1024]{2,1,0:T(8,128)(2,1)S(1)} all-gather(bf16[1,62,1024]{2,1,0:T(8,128)(2,1)S(1)} %bitcast.58), channel_id=1, replica_groups=mesh['groups'=2,'feat'=4,'tower'=4] {'tower'}, dimensions={0}, use_global_device_ids=true | all-gather | bytes 634880 | tf_op jit(solution)/shard_map/all_gather | solution.py:79
  261.3 0.1 reshape.30
  261.4 0.3 copy.27
  261.8 0.2 reshape.16
  261.9 0.3 convolution_multiply_fusion
  262.3 0.3 copy.28
  262.6 0.7 gather_fusion
  263.4 0.9 fusion.23
  (32 shorter events, 0.4 us)
Async XLA Ops:
  6.5 2.2 copy-start.1
  6.5 144.5 %all-gather.8.cloned.1.call-start = ((), (), s32[]{:S(2)}) async-start(), calls=%async_computation.2 | async-start | bytes 2621440 | tf_op jit(solution)/shard_map/all_gather | solution.py:53
  7.3 151.5 %all-gather.10.cloned.1.call-start = ((), (), s32[]{:S(2)}) async-start(), calls=%async_computation.3 | async-start | bytes 2621440 | tf_op jit(solution)/shard_map/all_gather | solution.py:58
  8.0 231.6 %all-gather.12.cloned.1.call-start = ((), (), s32[]{:S(2)}) async-start(), calls=%async_computation.4 | async-start | bytes 5242880 | tf_op jit(solution)/shard_map/all_gather | solution.py:59
  17.0 130.9 %all-to-all-start = ((bf16[1,4,1536,128]{3,1,0,2:T(4,128)(2,1)}), bf16[1,4,1536,128]{3,1,0,2:T(4,128)(2,1)S(1)}, u32[]{:S(2)}, u32[]{:S(2)}) async-start(bf16[1,4,1536,128]{3,1,0,2:T(4,128)(2,1)} %copy.25), calls=%async_computation | async-start | bytes 3145728 | tf_op jit(solution)/shard_map/all_to_all | solution.py:41
  26.9 60.8 %collective-permute-start = (bf16[1,4,384,128]{3,2,1,0:T(8,128)(2,1)}, bf16[1,4,384,128]{3,2,1,0:T(8,128)(2,1)S(1)}, u32[]{:S(2)}, u32[]{:S(2)}) collective-permute-start(bf16[1,4,384,128]{3,2,1,0:T(8,128)(2,1)} %get-tuple-element.7), channel_id=1, source_target_pairs={{0,12},{4,0},{8,4},{12,8},{1,13},{5,1},{9,5},{13,9},{2,14},{6,2},{... | collective-permute-start | bytes 1179656 | tf_op jit(solution)/shard_map/ppermute | solution.py:16
  30.8 111.5 %collective-permute-start.1 = (bf16[1,4,384,128]{3,2,1,0:T(8,128)(2,1)}, bf16[1,4,384,128]{3,2,1,0:T(8,128)(2,1)}, u32[]{:S(2)}, u32[]{:S(2)}) collective-permute-start(bf16[1,4,384,128]{3,2,1,0:T(8,128)(2,1)} %get-tuple-element.6), channel_id=1, source_target_pairs={{0,8},{4,12},{8,0},{12,4},{1,9},{5,13},{9,1},{13,5},{2,10},{6,14},... | collective-permute-start | bytes 1179656 | tf_op jit(solution)/shard_map/ppermute | solution.py:16
  30.8 112.5 %collective-permute-start.2 = (bf16[1,4,384,128]{3,2,1,0:T(8,128)(2,1)}, bf16[1,4,384,128]{3,2,1,0:T(8,128)(2,1)}, u32[]{:S(2)}, u32[]{:S(2)}) collective-permute-start(bf16[1,4,384,128]{3,2,1,0:T(8,128)(2,1)} %get-tuple-element.5), channel_id=1, source_target_pairs={{0,4},{4,8},{8,12},{12,0},{1,5},{5,9},{9,13},{13,1},{2,6},{6,10},{... | collective-permute-start | bytes 1179656 | tf_op jit(solution)/shard_map/ppermute | solution.py:16
  146.8 1.6 copy-start.5
  151.1 88.5 %copy-start = (bf16[384,128,32]{1,2,0:T(8,128)(2,1)S(1)}, bf16[384,128,32]{1,2,0:T(8,128)(2,1)}, u32[]{:S(2)}) copy-start(bf16[384,128,32]{1,2,0:T(8,128)(2,1)} %fusion.10) | copy-start | bytes 9437188
  151.1 88.5 %copy-start.7 = (f32[1,4096]{1,0:T(1,128)S(1)}, f32[1,4096]{1,0:T(1,128)}, u32[]{:S(2)}) copy-start(f32[1,4096]{1,0:T(1,128)} %param.18) | copy-start | bytes 49156
  151.1 88.5 %copy-start.8 = (f32[1,512]{1,0:T(1,128)S(1)}, f32[1,512]{1,0:T(1,128)}, u32[]{:S(2)}) copy-start(f32[1,512]{1,0:T(1,128)} %param.20) | copy-start | bytes 6148
  239.6 10.6 %copy-start.2 = (bf16[62,1024]{1,0:T(8,128)(2,1)S(1)}, bf16[62,1024]{1,0:T(8,128)(2,1)}, u32[]{:S(2)}) copy-start(bf16[62,1024]{1,0:T(8,128)(2,1)} %param.22) | copy-start | bytes 380932
  239.6 21.8 %copy-start.6 = (s32[120]{0:T(128)S(1)}, s32[120]{0:T(128)}, u32[]{:S(2)}) copy-start(s32[120]{0:T(128)} %constant.72) | copy-start | bytes 1444
  246.6 16.8 %copy-start.3 = (bf16[96,128]{1,0:T(8,128)(2,1)S(1)}, bf16[96,128]{1,0:T(8,128)(2,1)}, u32[]{:S(2)}) copy-start(bf16[96,128]{1,0:T(8,128)(2,1)} %param.21) | copy-start | bytes 73732
  246.6 16.8 %copy-start.4 = (f32[1024]{0:T(1024)S(1)}, f32[1024]{0:T(1024)}, u32[]{:S(2)}) copy-start(f32[1024]{0:T(1024)} %param.23) | copy-start | bytes 12292
  246.6 14.8 %all-to-all-start.1 = ((bf16[4,96,512]{2,1,0:T(8,128)(2,1)}), bf16[4,96,512]{2,1,0:T(8,128)(2,1)S(1)}, u32[]{:S(2)}, u32[]{:S(2)}) async-start(bf16[4,96,512]{2,1,0:T(8,128)(2,1)} %bitcast.12), calls=%async_computation.1 | async-start | bytes 786432 | tf_op jit(solution)/shard_map/all_to_all | solution.py:67
Sparse Core Ops, SparseCore 0:
  8.9 80.4 all-gather.7
  91.0 67.8 all-gather.9
  160.4 79.1 all-gather.11
